TPU v7x, 256 devices: a whole 4x4x8 slice. The times are simulated.
256 devices in a mesh: vgrp: 4 (over y), samp: 64 (over z, x, core).
Axes of the slice: x: 4, y: 4, z: 8, core: 2. Of those that a mesh axis runs over, the one named last changes fastest.
Arguments:
- phenotype: float32 [196608], P(('vgrp', 'samp')), may hold values from -6 to 6
- exposures: float32 [196608, 128], P('samp'), may hold values from -6 to 6
- perms: int32 [16, 196608], P(None, 'samp'), may hold values from 0 to 196607, each once within a row
- genotypes: int32 [196608, 2048], P('samp', 'vgrp'), may hold values from 0 to 2
Outputs:
- statistics: float32 [2048, 16], P(('vgrp', 'samp'))
Inputs may be any that keep to these rules, and one draw needn't show every extreme that they name: Each row of perms holds every sample index once.
All inputs are finite; a program needn't handle non-finite values.
Results may differ from a plain program's by a relative error of at most 0.00075.
Values sent between devices are 32-bit elements; how exact they have to be, the bound alone decides.
No kernel may reach another device: no remote copies, remote signals or barrier semaphores. Data moves between devices by JAX's collectives and lax.ppermute only.
A program may use at most 64 MiB of HBM per device.

v0:
```python
import jax
import jax.numpy as jnp
from jax import lax
from jax.sharding import PartitionSpec as P


def chol_solve(factor, rhs):
    middle = lax.linalg.triangular_solve(factor, rhs, left_side=True, lower=True)
    return lax.linalg.triangular_solve(factor, middle, left_side=True, lower=True, transpose_a=True)


def per_device(phenotype, exposures, perms, genotypes):
    hi = lax.Precision.HIGHEST
    nv = lax.axis_size("vgrp")
    local_rows = exposures.shape[0]
    width = exposures.shape[1]
    quarter = local_rows // nv
    offset_rows = lax.axis_index("vgrp") * quarter
    expo_part = lax.dynamic_slice_in_dim(exposures, offset_rows, quarter, 0)
    gram_part = jnp.dot(expo_part.T, expo_part, precision=hi)
    gram = lax.psum(gram_part, ("vgrp", "samp"))
    pheno_full = lax.all_gather(phenotype, ("vgrp", "samp"), axis=0, tiled=True)
    samples = pheno_full.shape[0]
    system = gram + 0.5 * samples * jnp.eye(width, dtype=jnp.float32)
    factor = jnp.linalg.cholesky(system)
    perm_part = lax.dynamic_slice_in_dim(perms, offset_rows, quarter, 1)
    pheno_part = jnp.take(pheno_full, perm_part.T, axis=0, mode="clip")
    cross_part = jnp.dot(expo_part.T, pheno_part, precision=hi)
    cross = lax.psum(cross_part, ("vgrp", "samp"))
    coefficients = chol_solve(factor, cross)
    permuted = lax.all_gather(pheno_part, "vgrp", axis=0, tiled=True)
    residuals = permuted - jnp.dot(exposures, coefficients, precision=hi)
    nperm = residuals.shape[1]
    weighted = (
        (exposures[:, :, None] * residuals[:, None, :])
        .reshape(local_rows, width * nperm)
        .astype(jnp.bfloat16)
    )
    dosages = genotypes.astype(jnp.bfloat16)
    partial = jnp.dot(dosages.T, weighted, preferred_element_type=jnp.float32)
    own_scores = lax.psum_scatter(partial, "samp", scatter_dimension=0, tiled=True)
    own_rows = own_scores.shape[0]
    shaped = own_scores.reshape(own_rows, width, nperm)
    return jnp.sum(shaped * shaped, axis=1) / (samples * width)


def solution(mesh):
    return jax.shard_map(
        per_device,
        mesh=mesh,
        in_specs=(P(("vgrp", "samp")), P("samp", None), P(None, "samp"), P("samp", "vgrp")),
        out_specs=P(("vgrp", "samp"), None),
        check_vma=False,
    )
```

profile of v0, /device:TPU:8, one launch (start us, length us, event | category | flops | bytes accessed | tf_op | source)
XLA Modules:
  0.0 509.8 jit_solution(5372724521363424822)
XLA Ops:
  6.5 2.6 fusion.4
  9.2 0.2 copy.17
  9.4 0.2 reshape.22
  9.6 0.7 reshape.31
  10.3 77.2 %all-gather.1 = f32[256,1,768]{2,1,0:T(1,128)S(1)} all-gather(f32[1,1,768]{2,1,0:T(1,128)S(1)} %reshape.31), channel_id=1, replica_groups=mesh['vgrp'=4,'samp'=64] {'vgrp','samp'}, dimensions={0}, use_global_device_ids=true | all-gather | bytes 789504 | tf_op jit(solution)/shard_map/all_gather | solution.py:22
  87.5 68.0 %gather_fusion = f32[12288]{0:T(1024)S(1)} fusion(f32[196608]{0:T(1024)S(1)} %bitcast.31, s32[12288]{0:T(1024)S(1)} %broadcast_clamp_fusion), kind=kCustom, calls=%fused_computation | custom fusion | bytes 147456 | tf_op jit(solution)/shard_map/jit(_take)/gather | solution.py:27
  155.5 0.2 reshape.21
  155.7 0.8 fusion.2
  156.4 0.1 copy.18
  156.6 12.1 %all-gather = f32[3072,16]{0,1:T(8,128)S(1)} all-gather(f32[768,16]{0,1:T(8,128)S(1)} %copy.18), channel_id=2, replica_groups=mesh['vgrp'=4,'samp'=64] {'vgrp'}, dimensions={0}, use_global_device_ids=true | all-gather | bytes 245760 | tf_op jit(solution)/shard_map/all_gather | solution.py:31
  168.7 0.5 copy.16
  169.2 72.9 %psum.15 = f32[128,16]{0,1:T(8,128)S(1)} all-reduce(f32[128,16]{0,1:T(8,128)S(1)} %fusion.2), channel_id=1, replica_groups=mesh['vgrp'=4,'samp'=64] {'vgrp','samp'}, use_global_device_ids=true, to_apply=%region_3.4 | all-reduce | flops 2048 | bytes 16384 | tf_op jit(solution)/shard_map/psum | solution.py:29
  242.1 14.6 %all-reduce.4.cloned.1.call-done = f32[128,128]{1,0:T(8,128)} async-done(((f32[128,128]{1,0:T(8,128)}), f32[128,128]{1,0:T(8,128)}) %all-reduce.4.cloned.1.call-update) | async-done | bytes 65552 | tf_op jit(solution)/shard_map/psum | solution.py:21
  256.7 1.5 select_add_fusion
  258.2 1.6 copy.19
  259.7 1.5 fusion.11
  261.2 13.2 %cholesky.16 = f32[128,128]{1,0:T(8,128)} custom-call(f32[128,128]{1,0:T(8,128)} %fusion.11), custom_call_target="Cholesky" | custom-call | tf_op jit(solution)/shard_map/jit(cholesky)/cholesky | solution.py:25
  274.4 0.9 select_reduce_fusion
  275.3 0.6 compare_reduce_fusion
  275.9 2.1 fusion.6
  278.0 11.3 %custom-call.8 = f32[1,128,128]{1,2,0:T(8,128)} custom-call(f32[1,128,128]{2,1,0:T(8,128)} %fusion.6), custom_call_target="InvertDiagBlocksLowerTriangular" | custom-call | tf_op jit(solution)/shard_map/triangular_solve | solution.py:9
  289.3 1.0 fusion.9
  290.3 1.0 fusion.7
  291.3 1.4 fusion
  292.8 3.4 multiply_convert_fusion
  296.2 10.8 %convolution_bitcast_fusion.1 = f32[512,2048]{0,1:T(8,128)} fusion(bf16[3072,2048]{0,1:T(8,128)(2,1)S(1)} %bitcast.32, s32[3072,512]{1,0:T(8,128)} %param.7), kind=kOutput, calls=%fused_computation.4 | convolution fusion | flops 6444023808 | bytes 23068672 | tf_op jit(solution)/shard_map/dot_general | solution.py:40
  307.0 0.6 copy-done.2
  307.7 0.6 dynamic-slice
  308.9 191.7 %all-reduce.6.cloned.1.call-done = f32[512,2048]{0,1:T(8,128)} async-done(((f32[512,2048]{0,1:T(8,128)}), f32[512,2048]{0,1:T(8,128)}) %all-reduce.6.cloned.1.call-update) | async-done | bytes 4194320
  500.6 1.6 dynamic-slice_multiply_fusion
  502.2 0.1 reduce_sum.9
  502.4 0.6 broadcast_multiply_fusion
  (12 shorter events, 0.2 us)
Async XLA Ops:
  6.5 2.6 copy-start
  6.5 250.1 %all-reduce.4.cloned.1.call-start = ((), (), s32[]{:S(2)}) async-start(), calls=%async_computation | async-start | bytes 131072 | tf_op jit(solution)/shard_map/psum | solution.py:21
  9.1 491.5 %all-reduce.6.cloned.1.call-start = ((), (), s32[]{:S(2)}) async-start(), calls=%async_computation.1 | async-start | bytes 8388608
  87.5 68.2 %copy-start.1 = (f32[3072,128]{1,0:T(8,128)S(1)}, f32[3072,128]{1,0:T(8,128)}, u32[]{:S(2)}) copy-start(f32[3072,128]{1,0:T(8,128)} %param.5) | copy-start | bytes 4718596
  307.0 0.7 copy-start.2
Sparse Core Ops, SparseCore 0:
  12.8 243.8 all-reduce.3
  307.1 193.4 all-reduce.5
where the time goes:
time: 511 us; the launch traced here: 510 us
  waiting for transfers between devices  206 us (40%)
  blocking collectives  162 us (32%)
  local copies, waits for them, and re-layouts  72.7 us (14%)
  other arithmetic  36.8 us (7%)
  matrix products  17.6 us (3%)
  between operations  14.2 us (3%)
    unnamed x3, waiting for transfers between devices  192 us
    all_gather x1, blocking collectives, per_device(): pheno_full = lax.all_gather(phenotype, ('vgrp', 'samp'), axis=0, tiled=True)  77.2 us
    psum x1, blocking collectives, per_device(): cross = lax.psum(cross_part, ('vgrp', 'samp'))  72.9 us
    gather x3, local copies, waits for them, and re-layouts, per_device(): pheno_part = jnp.take(pheno_full, perm_part.T, axis=0, mode='clip')  68.3 us
    another operation x3, other arithmetic, per_device(): factor = jnp.linalg.cholesky(system)  14.7 us
    psum x1, waiting for transfers between devices, per_device(): gram = lax.psum(gram_part, ('vgrp', 'samp'))  14.6 us
    another operation x2, other arithmetic, chol_solve(): lax.linalg.triangular_solve(factor, middle, left_side=True, lower=True, t...  13.4 us
    all_gather x1, blocking collectives, per_device(): permuted = lax.all_gather(pheno_part, 'vgrp', axis=0, tiled=True)  12.1 us
  transfers between devices with their start and end apart: 2, of which 2 were waited for; matrix products, arithmetic and copies ran while one was open for 14% of the time, Pallas kernels for 0%

commit v1 on v0

--- a/solution.py
+++ b/solution.py
@@ -2,6 +2,27 @@
 import jax.numpy as jnp
 from jax import lax
 from jax.sharding import PartitionSpec as P
+
+
+def gather_around(x, axis, dim):
+    peers, index, rows = (lax.axis_size(axis), lax.axis_index(axis), x.shape[dim])
+    upward = [(i, (i + 1) % peers) for i in range(peers)]
+    downward = [(i, (i - 1) % peers) for i in range(peers)]
+    whole = jnp.zeros((*x.shape[:dim], peers * rows, *x.shape[dim + 1 :]), x.dtype)
+    whole = lax.dynamic_update_slice_in_dim(whole, x, index * rows, axis=dim)
+    from_left = from_right = x
+    half = peers // 2
+    for step in range(1, half + 1):
+        from_left = lax.ppermute(from_left, axis, upward)
+        whole = lax.dynamic_update_slice_in_dim(
+            whole, from_left, (index - step) % peers * rows, axis=dim
+        )
+        if step < peers - half:
+            from_right = lax.ppermute(from_right, axis, downward)
+            whole = lax.dynamic_update_slice_in_dim(
+                whole, from_right, (index + step) % peers * rows, axis=dim
+            )
+    return whole
 
 
 def chol_solve(factor, rhs):
@@ -28,7 +49,7 @@
     cross_part = jnp.dot(expo_part.T, pheno_part, precision=hi)
     cross = lax.psum(cross_part, ("vgrp", "samp"))
     coefficients = chol_solve(factor, cross)
-    permuted = lax.all_gather(pheno_part, "vgrp", axis=0, tiled=True)
+    permuted = gather_around(pheno_part, "vgrp", 0)
     residuals = permuted - jnp.dot(exposures, coefficients, precision=hi)
     nperm = residuals.shape[1]
     weighted = (

time: 511 us -> 655 us (1.28)
  waiting for transfers between devices: 206 us -> 354 us
  blocking collectives: 162 us -> 152 us
    psum x1, waiting for transfers between devices: 14.6 us -> 161 us  [per_device(): gram = lax.psum(gram_part, ('vgrp', 'samp'))]
    all_gather x1 -> x0, blocking collectives: 12.1 us -> none  [per_device(): permuted = lax.all_gather(pheno_part, 'vgrp', axis=0, tiled=True)]
  transfers between devices with their start and end apart: 2 -> 5, of which waited for: 2 -> 3; matrix products, arithmetic and copies ran while one was open for 14% -> 6% of each run, Pallas kernels for 0% -> 0%
where the time goes in v1:
time: 655 us; the launch traced here: 654 us
  waiting for transfers between devices  354 us (54%)
  blocking collectives  152 us (23%)
  local copies, waits for them, and re-layouts  76.7 us (12%)
  other arithmetic  36.8 us (6%)
  matrix products  16.4 us (3%)
  between operations  14.2 us (2%)
    unnamed x3, waiting for transfers between devices  192 us
    psum x1, waiting for transfers between devices, per_device(): gram = lax.psum(gram_part, ('vgrp', 'samp'))  161 us
    all_gather x1, blocking collectives, per_device(): pheno_full = lax.all_gather(phenotype, ('vgrp', 'samp'), axis=0, tiled=True)  77.2 us
    psum x1, blocking collectives, per_device(): cross = lax.psum(cross_part, ('vgrp', 'samp'))  74.8 us
    gather x3, local copies, waits for them, and re-layouts, per_device(): pheno_part = jnp.take(pheno_full, perm_part.T, axis=0, mode='clip')  68.9 us
    another operation x3, other arithmetic, per_device(): factor = jnp.linalg.cholesky(system)  14.7 us
    another operation x2, other arithmetic, chol_solve(): lax.linalg.triangular_solve(factor, middle, left_side=True, lower=True, t...  13.4 us
  transfers between devices with their start and end apart: 5, of which 3 were waited for; matrix products, arithmetic and copies ran while one was open for 6% of the time, Pallas kernels for 0%

profile of v1, /device:TPU:8, one launch (start us, length us, event | category | flops | bytes accessed | tf_op | source)
XLA Modules:
  0.0 654.0 jit_solution(635498410380469955)
XLA Ops:
  6.5 0.9 copy-done
  7.8 0.7 reshape.30
  8.5 77.2 %all-gather = f32[256,1,768]{2,1,0:T(1,128)S(1)} all-gather(f32[1,1,768]{2,1,0:T(1,128)S(1)} %reshape.30), channel_id=1, replica_groups=mesh['vgrp'=4,'samp'=64] {'vgrp','samp'}, dimensions={0}, use_global_device_ids=true | all-gather | bytes 789504 | tf_op jit(solution)/shard_map/all_gather | solution.py:43
  85.7 68.0 %gather_fusion = f32[12288]{0:T(1024)S(1)} fusion(f32[196608]{0:T(1024)S(1)} %bitcast.31, s32[12288]{0:T(1024)S(1)} %broadcast_clamp_fusion), kind=kCustom, calls=%fused_computation | custom fusion | bytes 147456 | tf_op jit(solution)/shard_map/jit(_take)/gather | solution.py:48
  153.9 0.8 copy.22
  154.7 1.3 collective-permute-start
  155.9 0.8 collective-permute-start.1
  156.7 1.4 fusion.4
  158.2 0.8 fusion.2
  159.0 0.8 constant_dynamic-update-slice_fusion.3
  160.3 74.8 %psum.15 = f32[128,16]{0,1:T(8,128)S(1)} all-reduce(f32[128,16]{0,1:T(8,128)S(1)} %fusion.2), channel_id=1, replica_groups=mesh['vgrp'=4,'samp'=64] {'vgrp','samp'}, use_global_device_ids=true, to_apply=%region_3.4 | all-reduce | flops 2048 | bytes 16384 | tf_op jit(solution)/shard_map/psum | solution.py:50
  235.1 161.2 %all-reduce.4.cloned.1.call-done = f32[128,128]{1,0:T(8,128)} async-done(((f32[128,128]{1,0:T(8,128)}), f32[128,128]{1,0:T(8,128)}) %all-reduce.4.cloned.1.call-update) | async-done | bytes 65552 | tf_op jit(solution)/shard_map/psum | solution.py:42
  396.3 1.5 select_add_fusion
  397.7 1.6 copy.25
  399.3 1.5 fusion.11
  400.8 13.2 %cholesky.16 = f32[128,128]{1,0:T(8,128)} custom-call(f32[128,128]{1,0:T(8,128)} %fusion.11), custom_call_target="Cholesky" | custom-call | tf_op jit(solution)/shard_map/jit(cholesky)/cholesky | solution.py:46
  414.0 0.9 select_reduce_fusion
  414.8 0.6 compare_reduce_fusion
  415.5 2.1 fusion.6
  417.6 11.3 %custom-call.8 = f32[1,128,128]{1,2,0:T(8,128)} custom-call(f32[1,128,128]{2,1,0:T(8,128)} %fusion.6), custom_call_target="InvertDiagBlocksLowerTriangular" | custom-call | tf_op jit(solution)/shard_map/triangular_solve | solution.py:30
  428.9 1.0 fusion.9
  429.9 1.0 fusion.7
  430.9 1.7 collective-permute-start.2
  432.7 0.8 constant_dynamic-update-slice_fusion.2
  433.5 0.8 constant_dynamic-update-slice_fusion.1
  434.3 1.2 collective-permute-done.2
  435.5 1.4 fusion
  436.9 3.4 multiply_convert_fusion
  440.4 10.8 %convolution_bitcast_fusion.1 = f32[512,2048]{0,1:T(8,128)} fusion(bf16[3072,2048]{0,1:T(8,128)(2,1)S(1)} %bitcast.32, s32[3072,512]{1,0:T(8,128)} %param.7), kind=kOutput, calls=%fused_computation.4 | convolution fusion | flops 6444023808 | bytes 23068672 | tf_op jit(solution)/shard_map/dot_general | solution.py:61
  451.2 0.6 copy-done.2
  453.1 191.7 %all-reduce.6.cloned.1.call-done = f32[512,2048]{0,1:T(8,128)} async-done(((f32[512,2048]{0,1:T(8,128)}), f32[512,2048]{0,1:T(8,128)}) %all-reduce.6.cloned.1.call-update) | async-done | bytes 4194320
  644.8 1.6 dynamic-slice_multiply_fusion
  (22 shorter events, 2.5 us)
Async XLA Ops:
  6.5 0.9 copy-start
  6.5 389.7 %all-reduce.4.cloned.1.call-start = ((), (), s32[]{:S(2)}) async-start(), calls=%async_computation | async-start | bytes 131072 | tf_op jit(solution)/shard_map/psum | solution.py:42
  85.7 71.0 %copy-start.1 = (f32[3072,128]{1,0:T(8,128)S(1)}, f32[3072,128]{1,0:T(8,128)}, u32[]{:S(2)}) copy-start(f32[3072,128]{1,0:T(8,128)} %param.5) | copy-start | bytes 4718596
  154.7 276.2 %collective-permute-start = (f32[768,16]{0,1:T(8,128)}, f32[768,16]{0,1:T(8,128)}, u32[]{:S(2)}, u32[]{:S(2)}) collective-permute-start(f32[768,16]{0,1:T(8,128)} %copy.22), channel_id=1, source_target_pairs={{0,64},{64,128},{128,192},{192,0},{1,65},{65,129},{129,193},{193,1... | collective-permute-start | bytes 147464 | tf_op jit(solution)/shard_map/ppermute | solution.py:16
  155.9 277.6 %collective-permute-start.1 = (f32[768,16]{0,1:T(8,128)}, f32[768,16]{0,1:T(8,128)}, u32[]{:S(2)}, u32[]{:S(2)}) collective-permute-start(f32[768,16]{0,1:T(8,128)} %copy.22), channel_id=1, source_target_pairs={{0,192},{64,0},{128,64},{192,128},{1,193},{65,1},{129,65},{193,129... | collective-permute-start | bytes 147464 | tf_op jit(solution)/shard_map/ppermute | solution.py:21
  158.1 486.6 %all-reduce.6.cloned.1.call-start = ((), (), s32[]{:S(2)}) async-start(), calls=%async_computation.1 | async-start | bytes 8388608
  430.9 4.6 collective-permute-start.2
  451.2 0.7 copy-start.2
Sparse Core Ops, SparseCore 0:
  158.3 237.9 all-reduce.3
  451.3 193.3 all-reduce.5

commit v2 on v0

--- a/solution.py
+++ b/solution.py
@@ -26,7 +26,7 @@
     perm_part = lax.dynamic_slice_in_dim(perms, offset_rows, quarter, 1)
     pheno_part = jnp.take(pheno_full, perm_part.T, axis=0, mode="clip")
     cross_part = jnp.dot(expo_part.T, pheno_part, precision=hi)
-    cross = lax.psum(cross_part, ("vgrp", "samp"))
+    cross = jnp.sum(lax.all_gather(cross_part, ("vgrp", "samp")), axis=0)
     coefficients = chol_solve(factor, cross)
     permuted = lax.all_gather(pheno_part, "vgrp", axis=0, tiled=True)
     residuals = permuted - jnp.dot(exposures, coefficients, precision=hi)

time: 511 us -> 584 us (1.14)
  waiting for transfers between devices: 206 us -> 360 us
  blocking collectives: 162 us -> 89.5 us
  other arithmetic: 36.8 us -> 30.7 us
    all_gather x0 -> x1, waiting for transfers between devices: none -> 81.3 us  [per_device(): cross = jnp.sum(lax.all_gather(cross_part, ('vgrp', 'samp')), axis=0)]
    psum x1 -> x0, blocking collectives: 72.9 us -> none  [per_device(): cross = lax.psum(cross_part, ('vgrp', 'samp'))]
    psum x1, waiting for transfers between devices: 14.6 us -> 85.5 us  [per_device(): gram = lax.psum(gram_part, ('vgrp', 'samp'))]
    unnamed x3 -> x4, waiting for transfers between devices: 192 us -> 194 us
  transfers between devices with their start and end apart: 2 -> 3, of which waited for: 2 -> 3; matrix products, arithmetic and copies ran while one was open for 14% -> 17% of each run, Pallas kernels for 0% -> 0%
where the time goes in v2:
time: 584 us
  waiting for transfers between devices  360 us (62%)
  blocking collectives  89.5 us (15%)
  local copies, waits for them, and re-layouts  74.5 us (13%)
  other arithmetic  30.7 us (5%)
  matrix products  14.6 us (2%)
  between operations  13.9 us (2%)
    unnamed x4, waiting for transfers between devices  194 us
    psum x1, waiting for transfers between devices, per_device(): gram = lax.psum(gram_part, ('vgrp', 'samp'))  85.5 us
    all_gather x1, waiting for transfers between devices, per_device(): cross = jnp.sum(lax.all_gather(cross_part, ('vgrp', 'samp')), axis=0)  81.3 us
    all_gather x1, blocking collectives, per_device(): pheno_full = lax.all_gather(phenotype, ('vgrp', 'samp'), axis=0, tiled=True)  77.2 us
    gather x3, local copies, waits for them, and re-layouts, per_device(): pheno_part = jnp.take(pheno_full, perm_part.T, axis=0, mode='clip')  68.3 us
    another operation x3, other arithmetic, per_device(): factor = jnp.linalg.cholesky(system)  12.4 us
    all_gather x1, blocking collectives, per_device(): permuted = lax.all_gather(pheno_part, 'vgrp', axis=0, tiled=True)  12.3 us
  transfers between devices with their start and end apart: 3, of which 3 were waited for; matrix products, arithmetic and copies ran while one was open for 17% of the time, Pallas kernels for 0%

profile of v2, /device:TPU:8, one launch (start us, length us, event | category | flops | bytes accessed | tf_op | source)
XLA Modules:
  0.0 583.7 jit_solution(15229395256537473135)
XLA Ops:
  6.5 2.6 fusion.4
  9.2 0.2 copy.17
  9.4 0.2 reshape.22
  9.6 0.7 reshape.32
  10.2 77.2 %all-gather.2 = f32[256,1,768]{2,1,0:T(1,128)S(1)} all-gather(f32[1,1,768]{2,1,0:T(1,128)S(1)} %reshape.32), channel_id=1, replica_groups=mesh['vgrp'=4,'samp'=64] {'vgrp','samp'}, dimensions={0}, use_global_device_ids=true | all-gather | bytes 789504 | tf_op jit(solution)/shard_map/all_gather | solution.py:22
  87.4 68.0 %gather_fusion = f32[12288]{0:T(1024)S(1)} fusion(f32[196608]{0:T(1024)S(1)} %bitcast.36, s32[12288]{0:T(1024)S(1)} %broadcast_clamp_fusion), kind=kCustom, calls=%fused_computation | custom fusion | bytes 147456 | tf_op jit(solution)/shard_map/jit(_take)/gather | solution.py:27
  155.5 0.2 reshape.21
  155.7 1.4 fusion.2
  157.1 0.1 copy.18
  157.2 1.6 copy.16
  158.9 12.3 %all-gather = f32[3072,16]{0,1:T(8,128)S(1)} all-gather(f32[768,16]{0,1:T(8,128)S(1)} %copy.18), channel_id=2, replica_groups=mesh['vgrp'=4,'samp'=64] {'vgrp'}, dimensions={0}, use_global_device_ids=true | all-gather | bytes 245760 | tf_op jit(solution)/shard_map/all_gather | solution.py:31
  171.2 85.5 %all-reduce.4.cloned.1.call-done = f32[128,128]{1,0:T(8,128)} async-done(((f32[128,128]{1,0:T(8,128)}), f32[128,128]{1,0:T(8,128)}) %all-reduce.4.cloned.1.call-update) | async-done | bytes 65552 | tf_op jit(solution)/shard_map/psum | solution.py:21
  256.6 0.9 select_add_fusion
  257.6 0.9 fusion.11
  258.4 11.7 %cholesky.16 = f32[128,128]{1,0:T(8,128)S(1)} custom-call(f32[128,128]{1,0:T(8,128)S(1)} %fusion.11), custom_call_target="Cholesky" | custom-call | tf_op jit(solution)/shard_map/jit(cholesky)/cholesky | solution.py:25
  270.2 0.6 compare_reduce_fusion
  270.8 0.7 fusion.6
  271.5 9.8 %custom-call.8 = f32[1,128,128]{1,2,0:T(8,128)S(1)} custom-call(f32[1,128,128]{2,1,0:T(8,128)S(1)} %fusion.6), custom_call_target="InvertDiagBlocksLowerTriangular" | custom-call | tf_op jit(solution)/shard_map/triangular_solve | solution.py:9
  281.3 81.3 %all-gather.5.cloned.1.call-done = f32[32768,16]{0,1:T(8,128)} async-done(((f32[128,16]{0,1:T(8,128)}), f32[32768,16]{0,1:T(8,128)}) %all-gather.5.cloned.1.call-update) | async-done | bytes 2097168 | tf_op jit(solution)/shard_map/all_gather | solution.py:29
  362.6 2.1 copy.23
  364.8 0.1 bitcast_reduce_fusion
  364.9 0.2 fusion.9
  365.0 0.2 fusion.7
  365.2 1.4 fusion
  366.7 3.7 multiply_convert_fusion
  370.5 8.9 %convolution_bitcast_fusion.1 = f32[512,2048]{0,1:T(8,128)} fusion(bf16[3072,2048]{0,1:T(8,128)(2,1)S(1)} %bitcast.37, s32[3072,512]{1,0:T(8,128)S(1)} %bitcast.41), kind=kOutput, calls=%fused_computation.4 | convolution fusion | flops 6444023808 | bytes 23068672 | tf_op jit(solution)/shard_map/dot_general | solution.py:40
  379.4 0.6 copy-done.3
  380.1 0.6 dynamic-slice
  381.3 193.5 %all-reduce.6.cloned.1.call-done = f32[512,2048]{0,1:T(8,128)} async-done(((f32[512,2048]{0,1:T(8,128)}), f32[512,2048]{0,1:T(8,128)}) %all-reduce.6.cloned.1.call-update) | async-done | bytes 4194320
  574.8 1.6 dynamic-slice_multiply_fusion
  576.3 0.1 reduce_sum.19
  576.6 0.6 broadcast_multiply_fusion
  (23 shorter events, 0.4 us)
Async XLA Ops:
  6.5 2.6 copy-start
  6.5 250.1 %all-reduce.4.cloned.1.call-start = ((), (), s32[]{:S(2)}) async-start(), calls=%async_computation | async-start | bytes 131072 | tf_op jit(solution)/shard_map/psum | solution.py:21
  9.1 353.5 %all-gather.5.cloned.1.call-start = ((), (), s32[]{:S(2)}) async-start(), calls=%async_computation.1 | async-start | bytes 2105344 | tf_op jit(solution)/shard_map/all_gather | solution.py:29
  87.4 68.2 %copy-start.1 = (f32[3072,128]{1,0:T(8,128)S(1)}, f32[3072,128]{1,0:T(8,128)}, u32[]{:S(2)}) copy-start(f32[3072,128]{1,0:T(8,128)} %param.5) | copy-start | bytes 4718596
  157.1 417.7 %all-reduce.6.cloned.1.call-start = ((), (), s32[]{:S(2)}) async-start(), calls=%async_computation.2 | async-start | bytes 8388608
  362.6 4.1 copy-start.2
  362.6 7.8 %slice-start = ((s8[6291456]{0:T(1024)(128)(4,1)}), s8[4194304]{0:T(1024)(128)(4,1)S(1)}, s32[]{:S(2)}) async-start(s8[6291456]{0:T(1024)(128)(4,1)} %bitcast.40), calls=%async_computation.3 | async-start | bytes 8388608
  366.7 3.7 slice-start.1
  379.4 0.7 copy-start.3
Sparse Core Ops, SparseCore 0:
  12.8 243.7 all-reduce.3
  260.4 102.1 all-gather.4
  379.5 195.2 all-reduce.5
